TPU v7x, 256 devices: a whole 4x4x8 slice. The times are simulated.
256 devices in a mesh: row: 8 (over y, core), col: 8 (over z_hi, x), page: 4 (over z_lo).
Axes of the slice: x: 4, y: 4, z: 8 (z_hi: 2, z_lo: 4; z = z_hi * 4 + z_lo), core: 2. Of those that a mesh axis runs over, the one named last changes fastest.
Arguments:
- tokens: bfloat16 [32, 512, 2048], P(('row', 'page'), None, 'col'), may hold values from -6 to 6
- lengths: int32 [32], P(('row', 'page')), may hold values from 1 to 512, 4096 in all
- page_slot: int32 [32, 4], P('row'), may hold values from 0 to 15, as said below
- w_query: float32 [2048, 1024], P(('row', 'page'), 'col'), may hold values from -0.125 to 0.125
- w_keyval: float32 [2, 2048, 256], P(None, ('row', 'page')), may hold values from -0.125 to 0.125
- w_out: float32 [1024, 2048], P('col', ('row', 'page')), may hold values from -0.1875 to 0.1875
- w_gateup: float32 [2, 2048, 5120], P(None, ('row', 'page'), 'col'), may hold values from -0.125 to 0.125
- w_down: float32 [5120, 2048], P('col', ('row', 'page')), may hold values from -0.078125 to 0.078125
- attn_gain: float32 [2048], replicated, may hold values from 0.1 to 1.9
- ffn_gain: float32 [2048], replicated, may hold values from 0.1 to 1.9
- query_gain: float32 [64], replicated, may hold values from 0.1 to 1.9
- key_gain: float32 [64], replicated, may hold values from 0.1 to 1.9
Outputs:
- layer_out: bfloat16 [32, 512, 2048], P(('row', 'page'), None, 'col')
- kv_pages: bfloat16 [2, 128, 128, 1024], P(None, ('row', 'page'), None, 'col')
Inputs may be any that keep to these rules, and one draw needn't show every extreme that they name: `lengths`: each prompt's real tokens; in every draw some prompt has exactly 512. `page_slot`: within the prompts of one index of row the values are a permutation; page v belongs to index v // 4 of page; the 4 blocks of the prompts of one device send the same number of blocks to each of the 4 indices of page.
All inputs are finite; a program needn't handle non-finite values. No bound on the sum of `lengths` on one device may be relied on, other than what follows from the above.
Results may differ from a plain program's by a relative error of at most 0.012.
Values may be sent and summed in bfloat16 or wider, within the bound.
No kernel may reach another device: no remote copies, remote signals or barrier semaphores. Data moves between devices by JAX's collectives and lax.ppermute only.
A program may use at most 64 MiB of HBM per device.

v0:
```python
import jax
import jax.numpy as jnp
from jax import lax
from jax.sharding import PartitionSpec as P

PAGE_LEN = 128


def normalize(values, norm_gain):
    mean_sq = jnp.mean(values * values, axis=-1, keepdims=True)
    return values * lax.rsqrt(mean_sq + 1e-06) * norm_gain


def rotate(values):
    row_count = values.shape[-3]
    head_dim = values.shape[-1]
    half_dim = head_dim // 2
    frequency = 10000.0 ** (-2.0 * jnp.arange(half_dim, dtype=jnp.float32) / head_dim)
    angles = jnp.arange(row_count, dtype=jnp.float32)[:, None] * frequency[None, :]
    cosine = jnp.cos(angles)[:, None, :]
    sine_table = jnp.sin(angles)[:, None, :]
    leading = values[..., :half_dim]
    trailing = values[..., half_dim:]
    return jnp.concatenate(
        [leading * cosine - trailing * sine_table, trailing * cosine + leading * sine_table],
        axis=-1,
    )


def attend(query_rows, key_rows, value_rows, length):
    row_count = query_rows.shape[0]
    scores = jnp.einsum(
        "qhd,khd->hqk", query_rows, key_rows, preferred_element_type=jnp.float32
    ) * query_rows.shape[2] ** (-0.5)
    positions = jnp.arange(row_count, dtype=jnp.int32)
    seen_keys = (positions[None, :] <= positions[:, None]) & (positions[None, :] < length)
    exp_scores = jnp.where(seen_keys[None], jnp.exp(scores), 0.0)
    attn_probs = (exp_scores / jnp.sum(exp_scores, axis=-1, keepdims=True)).astype(jnp.bfloat16)
    attended = jnp.einsum(
        "hqk,khd->qhd", attn_probs, value_rows, preferred_element_type=jnp.float32
    )
    live_rows = (positions < length)[:, None, None]
    return jnp.where(live_rows, attended, 0.0).astype(jnp.bfloat16)


def on_device(
    tokens,
    lengths,
    page_slot,
    w_query,
    w_keyval,
    w_out,
    w_gateup,
    w_down,
    attn_gain,
    ffn_gain,
    query_gain,
    key_gain,
):
    col_count = lax.axis_size("col")
    col_index = lax.axis_index("col")
    head_dim = query_gain.shape[0]
    local_width = w_query.shape[1]
    local_heads = local_width // head_dim
    kv_heads = w_keyval.shape[2] // head_dim
    group_size = local_heads * col_count // kv_heads
    kv_index = (col_index * local_heads + jnp.arange(local_heads, dtype=jnp.int32)) // group_size
    columns = (
        kv_index[:, None] * head_dim + jnp.arange(head_dim, dtype=jnp.int32)[None, :]
    ).reshape(-1)
    keyval_piece = w_keyval.astype(jnp.bfloat16)
    query_piece = w_query.astype(jnp.bfloat16)
    out_piece = w_out.astype(jnp.bfloat16)
    gateup_piece = w_gateup.astype(jnp.bfloat16)
    down_piece = w_down.astype(jnp.bfloat16)
    query_full, keyval_full, out_full, gateup_full, down_full = (
        lax.all_gather(query_piece, ("row", "page"), axis=0, tiled=True),
        lax.all_gather(keyval_piece, ("row", "page"), axis=1, tiled=True),
        lax.all_gather(out_piece, ("row", "page"), axis=1, tiled=True),
        lax.all_gather(gateup_piece, ("row", "page"), axis=1, tiled=True),
        lax.all_gather(down_piece, ("row", "page"), axis=1, tiled=True),
    )
    keyval_used = jnp.take(keyval_full, columns, axis=2)
    merged_qkv = jnp.concatenate([query_full, keyval_used[0], keyval_used[1]], axis=1)
    merged_gateup = jnp.concatenate([gateup_full[0], gateup_full[1]], axis=1)
    prompt_count, seq_len, local_feat = tokens.shape
    gathered = lax.all_gather(tokens, "col", axis=2, tiled=True)
    model_width = gathered.shape[2]
    attn_in = normalize(gathered.astype(jnp.float32), attn_gain).astype(jnp.bfloat16)
    projected = jnp.dot(
        attn_in.reshape(-1, model_width), merged_qkv, preferred_element_type=jnp.float32
    )
    projected = projected.reshape(prompt_count, seq_len, 3, local_heads, head_dim)
    queries = rotate(normalize(projected[:, :, 0], query_gain)).astype(jnp.bfloat16)
    keys_rot = rotate(normalize(projected[:, :, 1], key_gain)).astype(jnp.bfloat16)
    values_in = projected[:, :, 2].astype(jnp.bfloat16)
    attended_one = attend(queries[0], keys_rot[0], values_in[0], lengths[0])
    outputs = [attended_one.reshape(seq_len, local_width)]
    attended = jnp.stack(outputs)
    attn_terms = jnp.dot(
        attended.reshape(-1, local_width), out_full, preferred_element_type=jnp.float32
    )
    attn_terms = attn_terms.reshape(prompt_count, seq_len, model_width)
    attn_sum = lax.psum_scatter(
        attn_terms.astype(jnp.bfloat16), "col", scatter_dimension=2, tiled=True
    ).astype(jnp.float32)
    residual = (tokens.astype(jnp.float32) + attn_sum).astype(jnp.bfloat16)
    residual_all = lax.all_gather(residual, "col", axis=2, tiled=True)
    ffn_in = normalize(residual_all.astype(jnp.float32), ffn_gain).astype(jnp.bfloat16)
    gate_up = jnp.dot(
        ffn_in.reshape(-1, model_width), merged_gateup, preferred_element_type=jnp.float32
    )
    unit_count = gateup_full.shape[2]
    hidden = (jax.nn.silu(gate_up[:, :unit_count]) * gate_up[:, unit_count:]).astype(jnp.bfloat16)
    ffn_terms = jnp.dot(hidden, down_full, preferred_element_type=jnp.float32).reshape(
        prompt_count, seq_len, model_width
    )
    ffn_sum = lax.psum_scatter(
        ffn_terms.astype(jnp.bfloat16), "col", scatter_dimension=2, tiled=True
    ).astype(jnp.float32)
    layer_out = (residual.astype(jnp.float32) + ffn_sum).astype(jnp.bfloat16)
    page_count = lax.axis_size("page")
    page_index = lax.axis_index("page")
    blocks_each = prompt_count * (seq_len // PAGE_LEN)
    capacity = blocks_each // page_count
    owners = page_slot // blocks_each
    local_slot = page_slot % blocks_each
    same_owner = owners[:, :, None] == owners[:, None, :]
    earlier = (
        jnp.arange(blocks_each, dtype=jnp.int32)[None, :]
        < jnp.arange(blocks_each, dtype=jnp.int32)[:, None]
    )
    order_in = jnp.sum((same_owner & earlier[None]).astype(jnp.int32), axis=2)
    my_owners = lax.dynamic_index_in_dim(owners, page_index, 0, keepdims=False)
    my_order = lax.dynamic_index_in_dim(order_in, page_index, 0, keepdims=False)
    send_pos = my_owners * capacity + my_order
    live_rows = (jnp.arange(seq_len, dtype=jnp.int32)[None, :] < lengths[:, None])[:, :, None, None]
    page_keys = jnp.where(live_rows, keys_rot, jnp.zeros_like(keys_rot)).reshape(
        blocks_each, PAGE_LEN, local_width
    )
    page_values = jnp.where(live_rows, values_in, jnp.zeros_like(values_in)).reshape(
        blocks_each, PAGE_LEN, local_width
    )
    stacked = jnp.stack([page_keys, page_values])
    outgoing = jnp.zeros_like(stacked).at[:, send_pos].set(stacked)
    incoming = lax.all_to_all(outgoing, "page", split_axis=1, concat_axis=1, tiled=True)
    arrival_hit = (owners[:, None, :] == page_index) & (
        order_in[:, None, :] == jnp.arange(capacity, dtype=jnp.int32)[None, :, None]
    )
    arrival_slot = jnp.sum(jnp.where(arrival_hit, local_slot[:, None, :], 0), axis=2).reshape(
        blocks_each
    )
    kv_pages = jnp.zeros_like(incoming).at[:, arrival_slot].set(incoming)
    return (layer_out, kv_pages)


def solution(mesh):
    in_specs = (
        P(("row", "page"), None, "col"),
        P(("row", "page")),
        P("row", None),
        P(("row", "page"), "col"),
        P(None, ("row", "page"), None),
        P("col", ("row", "page")),
        P(None, ("row", "page"), "col"),
        P("col", ("row", "page")),
        P(),
        P(),
        P(),
        P(),
    )
    out_specs = (P(("row", "page"), None, "col"), P(None, ("row", "page"), None, "col"))
    return jax.shard_map(
        on_device, mesh=mesh, in_specs=in_specs, out_specs=out_specs, check_vma=False
    )
```

profile of v0, /device:TPU:8, one launch (start us, length us, event | category | flops | bytes accessed | tf_op | source)
XLA Modules:
  0.0 662.8 jit_solution(14260095701070087263)
XLA Ops:
  7.2 0.0 all-gather.6.cloned.1.call-start
  7.2 0.7 all-gather.6.cloned.1.call-update
  7.9 0.0 all-gather.8.cloned.1.call-start
  7.9 1.6 copy.63
  9.6 0.0 all-gather.8.cloned.1.call-update
  9.6 0.0 reduce-scatter.3.cloned.1.call-start
  9.7 0.1 iota_add_fusion
  9.7 0.1 add.172
  9.8 0.1 add.169
  9.9 0.8 convert_element_type.114
  11.3 0.8 convert_element_type.121
  12.2 0.3 fusion.42
  12.5 0.8 fusion.28
  13.3 82.1 %all_gather.22 = bf16[2048,128]{1,0:T(8,128)(2,1)} all-gather(bf16[64,128]{1,0:T(8,128)(2,1)S(1)} %convert_element_type.114), channel_id=1, replica_groups=mesh['row'=8,'col'=8,'page'=4] {'row','page'}, dimensions={0}, use_global_device_ids=true | all-gather | bytes 540672 | tf_op jit(solution)/shard_map/all_gather | solution.py:77
  95.5 68.6 %all_gather.24 = bf16[128,2048]{0,1:T(8,128)(2,1)} all-gather(bf16[128,64]{0,1:T(8,128)(2,1)S(1)} %convert_element_type.121), channel_id=1, replica_groups=mesh['row'=8,'col'=8,'page'=4] {'row','page'}, dimensions={1}, use_global_device_ids=true | all-gather | bytes 540672 | tf_op jit(solution)/shard_map/all_gather | solution.py:79
  164.1 2.1 fusion.4
  166.2 9.9 %all-gather.8.cloned.1.call-done = bf16[2,2048,256]{2,0,1:T(2,128)(2,1)} async-done(((bf16[2,64,256]{2,0,1:T(2,128)(2,1)}), bf16[2,2048,256]{2,0,1:T(2,128)(2,1)}) %all-gather.8.cloned.1.call-update) | async-done | bytes 2097168 | tf_op jit(solution)/shard_map/all_gather | solution.py:78
  176.1 7.6 %copy.52 = bf16[2,2048,256]{1,0,2:T(2,128)(2,1)S(1)} copy(bf16[2,2048,256]{2,0,1:T(2,128)(2,1)} %all-gather.8.cloned.1.call-done) | data formatting | bytes 4194304 | tf_op jit(solution)/shard_map/all_gather | solution.py:78
  183.6 2.7 gather_fusion
  186.3 1.0 fusion.27
  187.3 1.5 fusion.55
  188.8 0.9 copy.53
  189.7 0.9 copy.54
  190.6 0.2 maximum_bitcast_fusion
  190.8 1.7 copy.55
  192.5 3.1 fusion.23
  195.6 0.1 multiply_reduce_fusion
  195.8 0.1 multiply_multiply_fusion
  195.9 0.1 subtract_convert_fusion
  196.0 0.6 copy-done.11
  196.6 0.8 fusion.21
  197.4 0.7 fusion.26
  198.1 0.3 copy-done.2
  198.4 2.1 fusion.11
  200.5 0.0 all-gather.12.cloned.1.call-start
  200.6 0.7 convert_element_type.129
  201.3 0.0 all-gather.12.cloned.1.call-update
  201.3 0.0 all-gather.10.cloned.1.call-start
  201.4 98.7 %reduce-scatter.3.cloned.1.call-done = bf16[1,512,256]{2,1,0:T(8,128)(2,1)} async-done(((bf16[1,512,2048]{2,1,0:T(8,128)(2,1)}), bf16[1,512,256]{2,1,0:T(8,128)(2,1)}) %reduce-scatter.3.cloned.1.call-update) | async-done | bytes 262160 | tf_op jit(solution)/shard_map/reduce_scatter | solution.py:104
  300.1 1.7 add_convert_fusion.1
  301.8 0.0 all-gather.10.cloned.1.call-update
  301.8 0.0 all-gather.14.cloned.1.call-start
  301.9 0.6 convert_element_type.131
  302.6 0.2 reduce-scatter.5.cloned.1.call-start
  302.8 85.4 %all-gather.12.cloned.1.call-done = bf16[2,2048,640]{2,1,0:T(8,128)(2,1)} async-done(((bf16[2,64,640]{2,1,0:T(8,128)(2,1)}), bf16[2,2048,640]{2,1,0:T(8,128)(2,1)}) %all-gather.12.cloned.1.call-update) | async-done | bytes 5242896 | tf_op jit(solution)/shard_map/all_gather | solution.py:80
  388.2 4.6 slice_bitcast_fusion.1
  392.8 75.0 %all-gather.10.cloned.1.call-done = bf16[1,512,2048]{2,1,0:T(8,128)(2,1)} async-done(((bf16[1,512,256]{2,1,0:T(8,128)(2,1)}), bf16[1,512,2048]{2,1,0:T(8,128)(2,1)}) %all-gather.10.cloned.1.call-update) | async-done | bytes 2097168 | tf_op jit(solution)/shard_map/all_gather | solution.py:108
  467.8 2.2 fusion.7
  470.0 6.2 fusion
  476.2 76.6 %all-gather.14.cloned.1.call-done = bf16[640,2048]{0,1:T(8,128)(2,1)} async-done(((bf16[640,64]{0,1:T(8,128)(2,1)}), bf16[640,2048]{0,1:T(8,128)(2,1)}) %all-gather.14.cloned.1.call-update) | async-done | bytes 2621456 | tf_op jit(solution)/shard_map/all_gather | solution.py:81
  552.8 5.7 fusion.10
  558.6 0.6 copy-done.13
  559.2 0.2 convert_reduce_fusion
  559.6 0.1 copy.57
  559.8 0.1 copy.58
  559.9 0.1 broadcast_select_fusion.2
  560.1 0.8 scatter_fusion
  560.9 0.7 copy.59
  561.6 4.6 all-to-all-start
  566.3 0.1 fusion.44
  566.4 14.3 %all-to-all-done = bf16[2,4,128,128]{3,2,0,1:T(8,128)(2,1)S(1)} async-done(((bf16[2,4,128,128]{3,2,0,1:T(8,128)(2,1)}), bf16[2,4,128,128]{3,2,0,1:T(8,128)(2,1)S(1)}, u32[]{:S(2)}, u32[]{:S(2)}) %all-to-all-start) | async-done | bytes 262176 | tf_op jit(solution)/shard_map/all_to_all | solution.py:146
  580.7 0.8 scatter_fusion.1
  581.5 72.7 %reduce-scatter.5.cloned.1.call-done = bf16[1,512,256]{2,1,0:T(8,128)(2,1)} async-done(((bf16[1,512,2048]{2,1,0:T(8,128)(2,1)}), bf16[1,512,256]{2,1,0:T(8,128)(2,1)}) %reduce-scatter.5.cloned.1.call-update) | async-done | bytes 262160 | tf_op jit(solution)/shard_map/reduce_scatter | solution.py:118
  654.2 1.7 add_convert_fusion
  (58 shorter events, 0.4 us)
Async XLA Ops:
  7.2 156.9 %all-gather.6.cloned.1.call-start = ((), (), s32[]{:S(2)}) async-start(), calls=%async_computation.3 | async-start | bytes 2359296 | tf_op jit(solution)/shard_map/all_gather | solution.py:87
  7.9 168.2 %all-gather.8.cloned.1.call-start = ((), (), s32[]{:S(2)}) async-start(), calls=%async_computation.4 | async-start | bytes 2162688 | tf_op jit(solution)/shard_map/all_gather | solution.py:78
  9.6 290.5 %reduce-scatter.3.cloned.1.call-start = ((), (), s32[]{:S(2)}) async-start(), calls=%async_computation.5 | async-start | bytes 2359296 | tf_op jit(solution)/shard_map/reduce_scatter | solution.py:104
  188.8 1.7 copy-start.3
  190.8 1.7 copy-start.16
  192.5 3.3 copy-start.14
  192.5 3.3 copy-start.15
  195.6 1.0 copy-start.11
  195.9 1.4 copy-start.7
  196.0 1.4 copy-start.9
  197.4 1.0 copy-start.2
  198.4 2.2 copy-start.6
  198.4 101.7 %copy-start.4 = (bf16[1,512,256]{2,1,0:T(8,128)(2,1)S(1)}, bf16[1,512,256]{2,1,0:T(8,128)(2,1)}, u32[]{:S(2)}) copy-start(bf16[1,512,256]{2,1,0:T(8,128)(2,1)} %param.12) | copy-start | bytes 786436
  200.5 101.4 %copy-start.12 = (f32[640,64]{0,1:T(8,128)S(1)}, f32[640,64]{0,1:T(8,128)}, u32[]{:S(2)}) copy-start(f32[640,64]{0,1:T(8,128)} %param.19) | copy-start | bytes 491524
  200.5 187.7 %all-gather.12.cloned.1.call-start = ((), (), s32[]{:S(2)}) async-start(), calls=%async_computation.7 | async-start | bytes 5406720 | tf_op jit(solution)/shard_map/all_gather | solution.py:80
  201.3 266.4 %all-gather.10.cloned.1.call-start = ((), (), s32[]{:S(2)}) async-start(), calls=%async_computation.6 | async-start | bytes 2359296 | tf_op jit(solution)/shard_map/all_gather | solution.py:108
  301.8 251.0 %all-gather.14.cloned.1.call-start = ((), (), s32[]{:S(2)}) async-start(), calls=%async_computation.8 | async-start | bytes 2703360 | tf_op jit(solution)/shard_map/all_gather | solution.py:81
  302.6 351.6 %reduce-scatter.5.cloned.1.call-start = ((), (), s32[]{:S(2)}) async-start(), calls=%async_computation.9 | async-start | bytes 2359296 | tf_op jit(solution)/shard_map/reduce_scatter | solution.py:118
  392.8 77.2 %copy-start.17 = (f32[2048]{0:T(1024)S(1)}, f32[2048]{0:T(1024)}, u32[]{:S(2)}) copy-start(f32[2048]{0:T(1024)} %param.21) | copy-start | bytes 24580
  467.8 2.2 copy-start.1
  558.5 0.7 copy-start.13
  558.5 1.0 copy-start.8
  558.5 1.0 copy-start.10
  559.9 94.3 %copy-start = (bf16[1,512,256]{2,1,0:T(8,128)(2,1)S(1)}, bf16[1,512,256]{2,1,0:T(8,128)(2,1)}, u32[]{:S(2)}) copy-start(bf16[1,512,256]{2,1,0:T(8,128)(2,1)} %add_convert_fusion.1) | copy-start | bytes 786436
  561.6 19.1 %all-to-all-start = ((bf16[2,4,128,128]{3,2,0,1:T(8,128)(2,1)}), bf16[2,4,128,128]{3,2,0,1:T(8,128)(2,1)S(1)}, u32[]{:S(2)}, u32[]{:S(2)}) async-start(bf16[2,4,128,128]{3,2,0,1:T(8,128)(2,1)} %copy.59), calls=%async_computation.2 | async-start | bytes 524288 | tf_op jit(solution)/shard_map/all_to_all | solution.py:146
  581.5 74.4 %copy-start.5 = (bf16[2,4,128,128]{3,2,1,0:T(8,128)(2,1)}, bf16[2,4,128,128]{3,2,1,0:T(8,128)(2,1)S(1)}, u32[]{:S(2)}) copy-start(bf16[2,4,128,128]{3,2,1,0:T(8,128)(2,1)S(1)} %scatter_fusion.1) | copy-start | bytes 786436
Sparse Core Ops, SparseCore 0:
  10.4 74.3 all-gather.5
  87.2 88.8 all-gather.7
  200.7 99.3 reduce-scatter.2
  302.3 85.8 all-gather.11
  391.1 76.6 all-gather.9
  469.4 83.3 all-gather.13
  558.7 95.4 reduce-scatter.4
where the time goes:
time: 663 us
  waiting for transfers between devices  433 us (65%)
  blocking collectives  151 us (23%)
  local copies, waits for them, and re-layouts  25.8 us (4%)
  matrix products  18.6 us (3%)
  between operations  15.2 us (2%)
  other arithmetic  13.9 us (2%)
    reduce_scatter x1, waiting for transfers between devices, on_device(): lax.psum_scatter(attn_terms.astype(jnp.bfloat16), 'col', scatter_dimensio...  98.7 us
    all_gather x1, waiting for transfers between devices, on_device(): lax.all_gather(gateup_piece, ('row', 'page'), axis=1, tiled=True)  85.4 us
    all_gather x1, blocking collectives, on_device(): lax.all_gather(query_piece, ('row', 'page'), axis=0, tiled=True)  82.1 us
    all_gather x1, waiting for transfers between devices, on_device(): lax.all_gather(down_piece, ('row', 'page'), axis=1, tiled=True)  76.6 us
    all_gather x1, waiting for transfers between devices, on_device(): residual_all = lax.all_gather(residual, 'col', axis=2, tiled=True)  75 us
    reduce_scatter x1, waiting for transfers between devices, on_device(): lax.psum_scatter(ffn_terms.astype(jnp.bfloat16), 'col', scatter_dimension...  72.7 us
    all_gather x1, blocking collectives, on_device(): lax.all_gather(out_piece, ('row', 'page'), axis=1, tiled=True)  68.6 us
    all_to_all x1, waiting for transfers between devices, on_device(): lax.all_to_all(outgoing, 'page', split_axis=1, concat_axis=1, tiled=True)  14.3 us
  transfers between devices with their start and end apart: 8, of which 7 were waited for; matrix products, arithmetic and copies ran while one was open for 4% of the time, Pallas kernels for 0%

commit v1 on v0

--- a/solution.py
+++ b/solution.py
@@ -105,7 +105,10 @@
         attn_terms.astype(jnp.bfloat16), "col", scatter_dimension=2, tiled=True
     ).astype(jnp.float32)
     residual = (tokens.astype(jnp.float32) + attn_sum).astype(jnp.bfloat16)
-    residual_all = lax.all_gather(residual, "col", axis=2, tiled=True)
+    y_new = jax.lax.axis_size("col")
+    block_out = jnp.stack([residual] * y_new, axis=0)
+    back = jax.lax.all_to_all(block_out, "col", 0, 0)
+    residual_all = jnp.concatenate(back, axis=2)
     ffn_in = normalize(residual_all.astype(jnp.float32), ffn_gain).astype(jnp.bfloat16)
     gate_up = jnp.dot(
         ffn_in.reshape(-1, model_width), merged_gateup, preferred_element_type=jnp.float32

time: 663 us -> 624 us (0.941)
  waiting for transfers between devices: 433 us -> 388 us
    all_gather x1 -> x0, waiting for transfers between devices: 75 us -> none  [on_device(): residual_all = lax.all_gather(residual, 'col', axis=2, tiled=True)]
    all_gather x1, waiting for transfers between devices: 85.4 us -> 113 us  [on_device(): lax.all_gather(gateup_piece, ('row', 'page'), axis=1, tiled=True)]
  transfers between devices with their start and end apart: 8 -> 8, of which waited for: 7 -> 6; matrix products, arithmetic and copies ran while one was open for 4% -> 4% of each run, Pallas kernels for 0% -> 0%
where the time goes in v1:
time: 624 us
  waiting for transfers between devices  388 us (62%)
  blocking collectives  151 us (24%)
  local copies, waits for them, and re-layouts  30.4 us (5%)
  matrix products  16.9 us (3%)
  between operations  15.1 us (2%)
  other arithmetic  13.5 us (2%)
  starting transfers between devices  8.72 us (1%)
    all_gather x1, waiting for transfers between devices, on_device(): lax.all_gather(gateup_piece, ('row', 'page'), axis=1, tiled=True)  113 us
    reduce_scatter x1, waiting for transfers between devices, on_device(): lax.psum_scatter(attn_terms.astype(jnp.bfloat16), 'col', scatter_dimensio...  98.9 us
    all_gather x1, blocking collectives, on_device(): lax.all_gather(query_piece, ('row', 'page'), axis=0, tiled=True)  82.1 us
    all_gather x1, waiting for transfers between devices, on_device(): lax.all_gather(down_piece, ('row', 'page'), axis=1, tiled=True)  78.6 us
    reduce_scatter x1, waiting for transfers between devices, on_device(): lax.psum_scatter(ffn_terms.astype(jnp.bfloat16), 'col', scatter_dimension...  72.5 us
    all_gather x1, blocking collectives, on_device(): lax.all_gather(out_piece, ('row', 'page'), axis=1, tiled=True)  68.6 us
    all_to_all x1, waiting for transfers between devices, on_device(): lax.all_to_all(outgoing, 'page', split_axis=1, concat_axis=1, tiled=True)  14.3 us
  transfers between devices with their start and end apart: 8, of which 6 were waited for; matrix products, arithmetic and copies ran while one was open for 4% of the time, Pallas kernels for 0%

profile of v1, /device:TPU:8, one launch (start us, length us, event | category | flops | bytes accessed | tf_op | source)
XLA Modules:
  0.0 623.6 jit_solution(9426843928234597706)
XLA Ops:
  7.2 0.7 all-gather.5.cloned.1.call-update
  7.9 1.6 copy.70
  9.6 0.0 reduce-scatter.3.cloned.1.call-start
  9.7 0.1 iota_add_fusion
  9.7 0.1 add.172
  9.8 0.1 add.169
  9.9 0.8 convert_element_type.133
  11.3 0.8 convert_element_type.140
  12.2 0.3 fusion.38
  12.5 0.8 fusion.23
  13.3 82.1 %all_gather.19 = bf16[2048,128]{1,0:T(8,128)(2,1)} all-gather(bf16[64,128]{1,0:T(8,128)(2,1)S(1)} %convert_element_type.133), channel_id=1, replica_groups=mesh['row'=8,'col'=8,'page'=4] {'row','page'}, dimensions={0}, use_global_device_ids=true | all-gather | bytes 540672 | tf_op jit(solution)/shard_map/all_gather | solution.py:77
  95.5 68.6 %all_gather.21 = bf16[128,2048]{0,1:T(8,128)(2,1)} all-gather(bf16[128,64]{0,1:T(8,128)(2,1)S(1)} %convert_element_type.140), channel_id=1, replica_groups=mesh['row'=8,'col'=8,'page'=4] {'row','page'}, dimensions={1}, use_global_device_ids=true | all-gather | bytes 540672 | tf_op jit(solution)/shard_map/all_gather | solution.py:79
  164.1 2.1 fusion.4
  166.2 9.9 %all-gather.7.cloned.1.call-done = bf16[2,2048,256]{2,0,1:T(2,128)(2,1)} async-done(((bf16[2,64,256]{2,0,1:T(2,128)(2,1)}), bf16[2,2048,256]{2,0,1:T(2,128)(2,1)}) %all-gather.7.cloned.1.call-update) | async-done | bytes 2097168 | tf_op jit(solution)/shard_map/all_gather | solution.py:78
  176.1 7.6 %copy.57 = bf16[2,2048,256]{1,0,2:T(2,128)(2,1)S(1)} copy(bf16[2,2048,256]{2,0,1:T(2,128)(2,1)} %all-gather.7.cloned.1.call-done) | data formatting | bytes 4194304 | tf_op jit(solution)/shard_map/all_gather | solution.py:78
  183.6 2.7 gather_fusion
  186.3 1.0 fusion.22
  187.3 1.5 fusion.51
  188.8 0.9 copy.58
  189.7 0.9 copy.59
  190.6 0.2 maximum_bitcast_fusion
  190.8 1.6 copy.60
  192.5 3.2 fusion.18
  195.6 0.1 multiply_reduce_fusion.1
  195.7 0.1 multiply_multiply_fusion
  195.9 0.1 subtract_convert_fusion
  195.9 0.6 copy-done.8
  196.6 0.8 fusion.16
  197.3 0.7 fusion.21
  198.0 0.3 copy-done.3
  198.4 2.1 fusion.10
  200.5 0.0 all-gather.9.cloned.1.call-start
  200.6 0.7 convert_element_type.152
  201.3 98.9 %reduce-scatter.3.cloned.1.call-done = bf16[1,512,256]{2,1,0:T(8,128)(2,1)} async-done(((bf16[1,512,2048]{2,1,0:T(8,128)(2,1)}), bf16[1,512,256]{2,1,0:T(8,128)(2,1)}) %reduce-scatter.3.cloned.1.call-update) | async-done | bytes 262160 | tf_op jit(solution)/shard_map/reduce_scatter | solution.py:104
  300.2 1.0 fusion.34
  301.2 0.1 copy.62
  301.3 1.5 stack.4
  302.8 3.7 all-to-all-start
  306.5 1.6 convert_element_type.154
  308.1 0.2 reduce-scatter.5.cloned.1.call-start
  308.3 113.4 %all-gather.9.cloned.1.call-done = bf16[2,2048,640]{2,1,0:T(8,128)(2,1)} async-done(((bf16[2,64,640]{2,1,0:T(8,128)(2,1)}), bf16[2,2048,640]{2,1,0:T(8,128)(2,1)}) %all-gather.9.cloned.1.call-update) | async-done | bytes 5242896 | tf_op jit(solution)/shard_map/all_gather | solution.py:80
  421.7 5.3 slice_bitcast_fusion.1
  427.1 0.5 multiply_reduce_fusion
  427.6 0.6 bitcast_convert_fusion
  428.2 0.1 copy-done.9
  428.3 0.4 fusion.8
  428.7 1.3 copy-done
  430.0 0.8 copy-done.1
  430.8 4.4 fusion
  435.3 78.6 %all-gather.11.cloned.1.call-done = bf16[640,2048]{0,1:T(8,128)(2,1)} async-done(((bf16[640,64]{0,1:T(8,128)(2,1)}), bf16[640,2048]{0,1:T(8,128)(2,1)}) %all-gather.11.cloned.1.call-update) | async-done | bytes 2621456 | tf_op jit(solution)/shard_map/all_gather | solution.py:81
  513.8 5.7 fusion.9
  519.6 0.6 copy-done.10
  520.2 0.2 convert_reduce_fusion
  520.6 0.1 copy.64
  520.7 0.1 copy.65
  520.9 0.1 broadcast_select_fusion.2
  521.1 0.8 scatter_fusion
  521.9 0.7 copy.66
  522.6 4.6 all-to-all-start.1
  527.3 0.1 fusion.40
  527.4 14.3 %all-to-all-done.1 = bf16[2,4,128,128]{3,2,0,1:T(8,128)(2,1)S(1)} async-done(((bf16[2,4,128,128]{3,2,0,1:T(8,128)(2,1)}), bf16[2,4,128,128]{3,2,0,1:T(8,128)(2,1)S(1)}, u32[]{:S(2)}, u32[]{:S(2)}) %all-to-all-start.1) | async-done | bytes 262176 | tf_op jit(solution)/shard_map/all_to_all | solution.py:149
  541.7 0.8 scatter_fusion.1
  542.5 72.5 %reduce-scatter.5.cloned.1.call-done = bf16[1,512,256]{2,1,0:T(8,128)(2,1)} async-done(((bf16[1,512,2048]{2,1,0:T(8,128)(2,1)}), bf16[1,512,256]{2,1,0:T(8,128)(2,1)}) %reduce-scatter.5.cloned.1.call-update) | async-done | bytes 262160 | tf_op jit(solution)/shard_map/reduce_scatter | solution.py:121
  615.0 1.7 add_convert_fusion
  (53 shorter events, 0.6 us)
Async XLA Ops:
  7.2 156.9 %all-gather.5.cloned.1.call-start = ((), (), s32[]{:S(2)}) async-start(), calls=%async_computation.4 | async-start | bytes 2359296 | tf_op jit(solution)/shard_map/all_gather | solution.py:87
  7.9 168.2 %all-gather.7.cloned.1.call-start = ((), (), s32[]{:S(2)}) async-start(), calls=%async_computation.5 | async-start | bytes 2162688 | tf_op jit(solution)/shard_map/all_gather | solution.py:78
  9.6 290.6 %reduce-scatter.3.cloned.1.call-start = ((), (), s32[]{:S(2)}) async-start(), calls=%async_computation.6 | async-start | bytes 2359296 | tf_op jit(solution)/shard_map/reduce_scatter | solution.py:104
  188.8 1.7 copy-start.4
  190.8 1.7 copy-start.13
  192.5 3.3 copy-start.11
  192.5 3.3 copy-start.12
  195.6 1.0 copy-start.8
  197.3 1.0 copy-start.3
  198.4 2.2 copy-start.7
  198.4 101.8 %copy-start.2 = (bf16[1,512,256]{2,1,0:T(8,128)(2,1)S(1)}, bf16[1,512,256]{2,1,0:T(8,128)(2,1)}, u32[]{:S(2)}) copy-start(bf16[1,512,256]{2,1,0:T(8,128)(2,1)} %param.12) | copy-start | bytes 786436
  200.5 221.2 %all-gather.9.cloned.1.call-start = ((), (), s32[]{:S(2)}) async-start(), calls=%async_computation.7 | async-start | bytes 5406720 | tf_op jit(solution)/shard_map/all_gather | solution.py:80
  302.8 124.3 %all-to-all-start = ((bf16[8,1,512,256]{2,3,1,0:T(8,128)(2,1)}), bf16[8,1,512,256]{2,3,1,0:T(8,128)(2,1)S(1)}, u32[]{:S(2)}, u32[]{:S(2)}) async-start(bf16[8,1,512,256]{2,3,1,0:T(8,128)(2,1)} %stack.4), calls=%async_computation.1 | async-start | bytes 4194304 | tf_op jit(solution)/shard_map/all_to_all | solution.py:110
  306.5 207.4 %all-gather.11.cloned.1.call-start = ((), (), s32[]{:S(2)}) async-start(), calls=%async_computation.8 | async-start | bytes 2703360 | tf_op jit(solution)/shard_map/all_gather | solution.py:81
  308.1 306.9 %reduce-scatter.5.cloned.1.call-start = ((), (), s32[]{:S(2)}) async-start(), calls=%async_computation.9 | async-start | bytes 2359296 | tf_op jit(solution)/shard_map/reduce_scatter | solution.py:121
  427.6 0.7 copy-start.9
  428.3 1.7 copy-start
  428.3 2.5 copy-start.1
  519.5 0.7 copy-start.10
  520.9 94.1 %copy-start.5 = (bf16[1,512,256]{2,1,0:T(8,128)(2,1)S(1)}, bf16[1,512,256]{2,1,0:T(8,128)(2,1)}, u32[]{:S(2)}) copy-start(bf16[1,512,256]{2,1,0:T(8,128)(2,1)} %reduce-scatter.3.cloned.1.call-done) | copy-start | bytes 786436
  522.6 19.0 %all-to-all-start.1 = ((bf16[2,4,128,128]{3,2,0,1:T(8,128)(2,1)}), bf16[2,4,128,128]{3,2,0,1:T(8,128)(2,1)S(1)}, u32[]{:S(2)}, u32[]{:S(2)}) async-start(bf16[2,4,128,128]{3,2,0,1:T(8,128)(2,1)} %copy.66), calls=%async_computation.3 | async-start | bytes 524288 | tf_op jit(solution)/shard_map/all_to_all | solution.py:149
  542.5 74.3 %copy-start.6 = (bf16[2,4,128,128]{3,2,1,0:T(8,128)(2,1)}, bf16[2,4,128,128]{3,2,1,0:T(8,128)(2,1)S(1)}, u32[]{:S(2)}) copy-start(bf16[2,4,128,128]{3,2,1,0:T(8,128)(2,1)S(1)} %scatter_fusion.1) | copy-start | bytes 786436
Sparse Core Ops, SparseCore 0:
  10.4 74.3 all-gather.4
  87.2 88.8 all-gather.6
  200.6 99.4 reduce-scatter.2
  302.4 119.2 all-gather.8
  424.0 89.8 all-gather.10
  519.7 95.2 reduce-scatter.4
